TPU v7x, 32 devices: a whole 2x2x4 slice. The times are simulated.
32 devices in a mesh: req: 4 (over z), ctx: 8 (over y, x, core).
Axes of the slice: x: 2, y: 2, z: 4, core: 2. Of those that a mesh axis runs over, the one named last changes fastest.
Arguments:
- hidden_in: bfloat16 [4096, 2048], P(('req', 'ctx')), may hold values from -3 to 3
- queries: bfloat16 [4096, 1024], P(('req', 'ctx')), may hold values from -10 to 10
- span_keys: bfloat16 [4096, 1024], P(('req', 'ctx')), may hold values from -10 to 10
- span_values: bfloat16 [4096, 1024], P(('req', 'ctx')), may hold values from -6 to 6
- cache_keys: bfloat16 [6144, 1024], P(('req', 'ctx')), may hold values from -6 to 6
- cache_values: bfloat16 [6144, 1024], P(('req', 'ctx')), may hold values from -6 to 6
- cache_lengths: int32 [4], replicated, may hold values from 0 to 1536, as said below
- slot_request: int32 [4], replicated, may hold values from 0 to 3, each once
- out_weight: bfloat16 [1024, 2048], replicated, may hold values from -1.5 to 1.5
- norm_gain: float32 [2048], replicated, may hold values from 0.1 to 1.9
- expert_ids: int32 [4096, 8], P(('req', 'ctx')), may hold values from 0 to 15, all different within a row; in each aligned block of 128 rows (0 to 127, 128 to 255, ...) at most 128 rows name the same one
- expert_gates: float32 [4096, 8], P(('req', 'ctx')), may hold values from 0.05 to 0.5
- gate_proj: bfloat16 [16, 2048, 512], P('ctx'), may hold values from -0.125 to 0.125
- up_proj: bfloat16 [16, 2048, 512], P('ctx'), may hold values from -0.125 to 0.125
- down_proj: bfloat16 [16, 512, 2048], P('ctx'), may hold values from -0.25 to 0.25
Outputs:
- layer_out: bfloat16 [4096, 2048], P(('req', 'ctx'))
Inputs may be any that keep to these rules, and one draw needn't show every extreme that they name: `cache_lengths`: some request has exactly 1536 cached positions.
All inputs are finite; a program needn't handle non-finite values.
Results may differ from a plain program's by a relative error of at most 0.015.
Values may be sent and summed in bfloat16 or wider, within the bound.
No kernel may reach another device: no remote copies, remote signals or barrier semaphores. Data moves between devices by JAX's collectives and lax.ppermute only.
A program may use at most 192 MiB of HBM per device.

v0:
```python
import itertools
import math

import jax
import jax.numpy as jnp
from jax import lax
from jax.sharding import PartitionSpec as P

HEAD_DIM = 128


def attend_gathered(queries, span_keys, span_values, cache_keys, cache_values, length):
    token_count, column_count = queries.shape
    head_count = column_count // HEAD_DIM
    cached_rows = cache_keys.shape[0]
    block_rows = token_count + cached_rows
    scaling = 1.0 / math.sqrt(HEAD_DIM)
    key_block = jnp.concatenate([span_keys, cache_keys], 0)
    value_block = jnp.concatenate([span_values, cache_values], 0)
    piece_keys = lax.all_gather(key_block, "ctx", axis=0, tiled=True)
    piece_values = lax.all_gather(value_block, "ctx", axis=0, tiled=True)
    piece_rows = piece_keys.shape[0]
    index = jnp.arange(piece_rows, dtype=jnp.int32)
    owner = index // block_rows
    within = index % block_rows
    usable = (within < token_count) | (owner * cached_rows + within - token_count < length)
    scores = (
        jnp.einsum(
            "thd,phd->htp",
            queries.reshape(token_count, head_count, HEAD_DIM),
            piece_keys.reshape(piece_rows, head_count, HEAD_DIM),
            preferred_element_type=jnp.float32,
        )
        * scaling
    )
    scores = jnp.where(usable[None, None, :], scores, -1e30)
    peak = jnp.max(scores, axis=2, keepdims=True)
    weights = jnp.where(usable[None, None, :], jnp.exp(scores - peak), 0.0)
    total = jnp.sum(weights, axis=2)
    accum = jnp.einsum(
        "htp,phd->htd",
        weights.astype(jnp.bfloat16),
        piece_values.reshape(piece_rows, head_count, HEAD_DIM),
        preferred_element_type=jnp.float32,
    )
    return (
        (accum / total[:, :, None])
        .transpose(1, 0, 2)
        .reshape(token_count, column_count)
        .astype(jnp.bfloat16)
    )


def attend_by_head(queries, span_keys, span_values, cache_keys, cache_values, length, extra):
    token_count, column_count = queries.shape
    head_count = column_count // HEAD_DIM
    cached_rows = cache_keys.shape[0]
    ctx_count = lax.axis_size("ctx")
    local_heads = head_count // ctx_count
    width = local_heads * HEAD_DIM
    scaling = 1.0 / math.sqrt(HEAD_DIM)
    block_rows = token_count + cached_rows
    packed = jnp.concatenate(
        [queries, span_keys, cache_keys, span_values, cache_values], 0
    )
    base_rows = packed.shape[0]
    packed = jnp.concatenate([packed.reshape(base_rows, ctx_count, width), extra], 0)
    packed_rows = packed.shape[0]
    got = lax.all_to_all(packed, "ctx", split_axis=1, concat_axis=0, tiled=True)
    got = got.reshape(ctx_count, packed_rows, local_heads, HEAD_DIM)
    query_all = got[:, :token_count].reshape(ctx_count * token_count, local_heads, HEAD_DIM)
    key_all = got[:, token_count : token_count + block_rows].reshape(
        ctx_count * block_rows, local_heads, HEAD_DIM
    )
    extra_got = got[:, base_rows:]
    value_all = got[:, token_count + block_rows : base_rows].reshape(
        ctx_count * block_rows, local_heads, HEAD_DIM
    )
    piece_rows = ctx_count * block_rows
    index = jnp.arange(piece_rows, dtype=jnp.int32)
    owner = index // block_rows
    within = index % block_rows
    usable = (within < token_count) | (owner * cached_rows + within - token_count < length)
    scores = (
        jnp.einsum("thd,phd->htp", query_all, key_all, preferred_element_type=jnp.float32)
        * scaling
    )
    scores = jnp.where(usable[None, None, :], scores, -1e30)
    peak = jnp.max(scores, axis=2, keepdims=True)
    weights = jnp.where(usable[None, None, :], jnp.exp(scores - peak), 0.0)
    total = jnp.sum(weights, axis=2)
    accum = jnp.einsum(
        "htp,phd->thd",
        weights.astype(jnp.bfloat16),
        value_all,
        preferred_element_type=jnp.float32,
    )
    head_out = (accum / total.T[:, :, None]).astype(jnp.bfloat16)
    head_out = head_out.reshape(ctx_count, token_count, width)
    back = lax.all_to_all(head_out, "ctx", split_axis=0, concat_axis=0, tiled=True)
    return back.transpose(1, 0, 2).reshape(token_count, column_count), extra_got


def on_device(
    hidden_in,
    queries,
    span_keys,
    span_values,
    cache_keys,
    cache_values,
    cache_lengths,
    slot_request,
    out_weight,
    norm_gain,
    expert_ids,
    expert_gates,
    gate_proj,
    up_proj,
    down_proj,
):
    token_count, feature_width = hidden_in.shape
    column_count = queries.shape[1]
    head_count = column_count // HEAD_DIM
    ctx_count = lax.axis_size("ctx")
    slot_place = lax.axis_index("req")
    slot_count = slot_request.shape[0]
    slot_range = jnp.arange(slot_count, dtype=jnp.int32)
    request = jnp.sum(jnp.where(slot_range == slot_place, slot_request, 0))
    length = jnp.sum(jnp.where(slot_range == request, cache_lengths, 0))
    local_experts = gate_proj.shape[0]
    expert_total = local_experts * ctx_count
    gate_matrix = jnp.sum(
        jnp.where(
            expert_ids[:, :, None] == jnp.arange(expert_total, dtype=jnp.int32)[None, None, :],
            expert_gates[:, :, None],
            0.0,
        ),
        axis=1,
    )
    first_expert = lax.axis_index("ctx") * local_experts
    if head_count % ctx_count == 0:
        width = column_count // ctx_count
        high = lax.reduce_precision(gate_matrix, exponent_bits=8, mantissa_bits=7)
        rest = gate_matrix - high
        middle = lax.reduce_precision(rest, exponent_bits=8, mantissa_bits=7)
        low = rest - middle
        parts = jnp.stack([high, middle, low], -1).astype(jnp.bfloat16)
        parts = parts.reshape(token_count, ctx_count, local_experts * 3)
        parts = parts.transpose(1, 0, 2).reshape(ctx_count, -1)
        part_len = parts.shape[1]
        part_rows = -(-part_len // width)
        parts = jnp.pad(parts, ((0, 0), (0, part_rows * width - part_len)))
        parts = parts.reshape(ctx_count, part_rows, width).transpose(1, 0, 2)
        attended, parts_got = attend_by_head(
            queries, span_keys, span_values, cache_keys, cache_values, length, parts
        )
        parts_got = parts_got.reshape(ctx_count, part_rows * width)[:, :part_len]
        parts_got = parts_got.reshape(ctx_count * token_count, local_experts, 3).astype(
            jnp.float32
        )
        local_gates = (parts_got[:, :, 0] + parts_got[:, :, 1]) + parts_got[:, :, 2]
    else:
        attended = attend_gathered(
            queries, span_keys, span_values, cache_keys, cache_values, length
        )
        local_gates = lax.all_gather(
            lax.dynamic_slice_in_dim(gate_matrix, first_expert, local_experts, 1),
            "ctx",
            axis=0,
            tiled=True,
        )
    residual = hidden_in.astype(jnp.float32) + jnp.dot(
        attended, out_weight, preferred_element_type=jnp.float32
    )
    mean_square = jnp.mean(residual * residual, axis=1, keepdims=True)
    normed = (residual * lax.rsqrt(mean_square + 1e-06) * norm_gain).astype(jnp.bfloat16)

    def experts_on(rows, gates):
        moe = None
        for j in range(local_experts):
            gate_val = jnp.dot(rows, gate_proj[j], preferred_element_type=jnp.float32)
            up_val = jnp.dot(rows, up_proj[j], preferred_element_type=jnp.float32)
            activated = (jax.nn.silu(gate_val) * up_val).astype(jnp.bfloat16)
            activated = lax.optimization_barrier(activated)
            produced = jnp.dot(
                activated, down_proj[j], preferred_element_type=jnp.float32
            ).astype(jnp.bfloat16)
            term = gates[:, j : j + 1] * produced.astype(jnp.float32)
            moe = term if moe is None else moe + term
        return moe

    if ctx_count & (ctx_count - 1) == 0 and ctx_count > 1 and token_count % 2 == 0:
        me = lax.axis_index("ctx")
        half_rows = token_count // 2
        gate_blocks = local_gates.reshape(ctx_count, token_count, local_experts)
        orders = xor_orders(ctx_count)
        helds = gather_xor(
            [normed[h * half_rows : (h + 1) * half_rows] for h in range(2)], orders, ctx_count
        )
        parts = []
        for half, order in enumerate(orders):
            sources = jnp.array(relative_masks(order), jnp.int32) ^ me
            gates = jnp.take(
                gate_blocks[:, half * half_rows : (half + 1) * half_rows], sources, axis=0
            ).reshape(ctx_count * half_rows, local_experts)
            part = experts_on(helds[half].reshape(ctx_count * half_rows, feature_width), gates)
            parts.append(part.reshape(ctx_count, half_rows, feature_width))
        moe_halves = reduce_xor(parts, orders, ctx_count)
        moe_rows = jnp.concatenate(moe_halves, 0)
    else:
        normed_all = lax.all_gather(normed, "ctx", axis=0, tiled=True)
        moe = experts_on(normed_all, local_gates)
        moe_rows = lax.psum_scatter(
            moe.astype(jnp.bfloat16), "ctx", scatter_dimension=0, tiled=True
        ).astype(jnp.float32)
    final = (residual + moe_rows).astype(jnp.bfloat16)

    return route_to_request(final, slot_request)


def xor_orders(ctx_count):
    bits = ctx_count.bit_length() - 1
    first = list(range(bits - 1, -1, -1))
    second = list(first)
    if bits >= 3:
        second[0], second[1] = second[1], second[0]
    return [first, second]


def relative_masks(order):
    return [
        sum(((f >> step) & 1) << bit for step, bit in enumerate(order))
        for f in range(1 << len(order))
    ]


def swap(rows, mask, ctx_count):
    return lax.ppermute(rows, "ctx", [(c, c ^ mask) for c in range(ctx_count)])


def gather_xor(rows_list, orders, ctx_count):
    helds = [rows[None] for rows in rows_list]
    for step in range(len(orders[0])):
        helds = [
            jnp.concatenate([held, swap(held, 1 << order[step], ctx_count)], 0)
            for held, order in zip(helds, orders)
        ]
        helds = list(lax.optimization_barrier(tuple(helds)))
    return helds


def reduce_xor(parts, orders, ctx_count):
    totals = parts
    for step in reversed(range(len(orders[0]))):
        half = totals[0].shape[0] // 2
        sents = [
            swap(total[half:].astype(jnp.bfloat16), 1 << order[step], ctx_count)
            for total, order in zip(totals, orders)
        ]
        totals = [total[:half] + sent.astype(jnp.float32) for total, sent in zip(totals, sents)]
        totals = list(lax.optimization_barrier(tuple(totals)))
    return [total[0] for total in totals]


def route_to_request(final, slot_request):
    slot_count = slot_request.shape[0]
    token_count = final.shape[0]
    slot_range = jnp.arange(slot_count, dtype=jnp.int32)
    if slot_count <= 4:
        orders = list(itertools.permutations(range(slot_count)))
        table = jnp.array(orders, jnp.int32)
        match = jnp.all(table == slot_request[None, :], axis=1)
        choice = jnp.sum(jnp.where(match, jnp.arange(len(orders), dtype=jnp.int32), 0))

        def mover(order):
            pairs = [(g, order[g]) for g in range(slot_count)]
            if all(a == b for a, b in pairs):
                return lambda rows: rows
            return lambda rows: lax.ppermute(rows, "req", pairs)

        return lax.switch(choice, [mover(order) for order in orders], final)
    slot_place = lax.axis_index("req")
    source_slot = jnp.sum(jnp.where(slot_request == slot_place, slot_range, 0))
    piece = lax.all_gather(final, "req", axis=0, tiled=True)
    piece_rows = piece.shape[0]
    offset = source_slot * token_count
    inside = (offset >= 0) & (offset + token_count <= piece_rows)
    portion = lax.dynamic_slice_in_dim(
        piece, jnp.clip(offset, 0, piece_rows - token_count), token_count, 0
    )
    return jnp.where(inside, portion, jnp.zeros_like(final))


def solution(mesh):
    return jax.shard_map(
        on_device,
        mesh=mesh,
        in_specs=(
            P(("req", "ctx"), None),
            P(("req", "ctx"), None),
            P(("req", "ctx"), None),
            P(("req", "ctx"), None),
            P(("req", "ctx"), None),
            P(("req", "ctx"), None),
            P(),
            P(),
            P(),
            P(),
            P(("req", "ctx"), None),
            P(("req", "ctx"), None),
            P("ctx", None, None),
            P("ctx", None, None),
            P("ctx", None, None),
        ),
        out_specs=P(("req", "ctx"), None),
        check_vma=False,
    )
```

profile of v0, /device:TPU:0, one launch (start us, length us, event | category | flops | bytes accessed | tf_op | source)
XLA Modules:
  0.0 159.4 jit_solution(1065713197809723361)
XLA Ops:
  8.2 2.3 %copy.110 = bf16[774,8,128]{2,0,1:T(8,128)(2,1)} copy(bf16[774,8,128]{0,2,1:T(8,128)(2,1)S(1)} %pad_maximum_fusion.2) | data formatting | bytes 3170304 | tf_op jit(solution)/shard_map/concatenate | solution.py:67
  10.5 5.2 %all-to-all-start = ((bf16[774,8,128]{2,0,1:T(8,128)(2,1)}), bf16[774,8,128]{2,0,1:T(8,128)(2,1)S(1)}, u32[]{:S(2)}, u32[]{:S(2)}) async-start(bf16[774,8,128]{2,0,1:T(8,128)(2,1)} %copy.110), calls=%async_computation | async-start | bytes 3178496 | tf_op jit(solution)/shard_map/all_to_all | solution.py:69
  18.3 18.6 %all-to-all-done = bf16[774,8,128]{2,0,1:T(8,128)(2,1)S(1)} async-done(((bf16[774,8,128]{2,0,1:T(8,128)(2,1)}), bf16[774,8,128]{2,0,1:T(8,128)(2,1)S(1)}, u32[]{:S(2)}, u32[]{:S(2)}) %all-to-all-start) | async-done | bytes 1585184 | tf_op jit(solution)/shard_map/all_to_all | solution.py:69
  37.1 1.8 %fusion = (f32[1024]{0:T(1024)S(1)}, f32[1024,2560]{1,0:T(8,128)S(1)}) fusion(pred[2560]{0:T(1024)(128)(4,1)S(1)} %fusion.85, bf16[1024,128]{1,0:T(8,128)(2,1)S(1)} %bitcast.140, bf16[2560,128]{1,0:T(8,128)(2,1)S(1)} %bitcast.129), kind=kOutput, calls=%fused_computation.4 | convolution fusion | flops 678951936 | bytes 11409920 | tf_op jit(solution)/shard_map/thd,phd->htp/dot_general | solution.py:85
  38.9 2.7 %fusion.1 = f32[1024]{0:T(1024)S(1)} fusion(f32[1024,2560]{1,0:T(8,128)S(1)} %get-tuple-element.98, f32[1024]{0:T(1024)S(1)} %get-tuple-element.97, pred[2560]{0:T(1024)(128)(4,1)S(1)} %fusion.85), kind=kLoop, calls=%fused_computation.5 | loop fusion | flops 13106176 | bytes 10496512 | tf_op jit(solution)/shard_map/reduce_sum | solution.py:91
  41.6 3.0 %fusion.72 = bf16[16,8,8,128]{3,1,2,0:T(8,128)(2,1)S(1)} fusion(bf16[2560,128]{1,0:T(8,128)(2,1)S(1)} %bitcast.146, f32[1024,2560]{1,0:T(8,128)S(1)} %get-tuple-element.98, f32[1024]{0:T(1024)S(1)} %get-tuple-element.97, pred[2560]{0:T(1024)(128)(4,1)S(1)} %fusion.85, f32[1024]{0:T(1024)S(1)} %fusion.1), kind=kOutput, calls=%fused_computation.78 | convolution fusion | flops 684457984 | bytes 11414016 | tf_op jit(solution)/shard_map/htp,phd->thd/dot_general | solution.py:92
  45.4 3.6 %all-to-all-start.1 = ((bf16[8,128,128]{1,2,0:T(8,128)(2,1)}), bf16[8,128,128]{1,2,0:T(8,128)(2,1)S(1)}, u32[]{:S(2)}, u32[]{:S(2)}) async-start(bf16[8,128,128]{1,2,0:T(8,128)(2,1)} %copy.111), calls=%async_computation.1 | async-start | bytes 524288 | tf_op jit(solution)/shard_map/all_to_all | solution.py:100
  49.0 6.7 %all-to-all-done.1 = bf16[8,128,128]{1,2,0:T(8,128)(2,1)S(1)} async-done(((bf16[8,128,128]{1,2,0:T(8,128)(2,1)}), bf16[8,128,128]{1,2,0:T(8,128)(2,1)S(1)}, u32[]{:S(2)}, u32[]{:S(2)}) %all-to-all-start.1) | async-done | bytes 262176 | tf_op jit(solution)/shard_map/all_to_all | solution.py:100
  55.7 3.0 %multiply_reduce_fusion = (f32[128]{0:T(128)S(1)}, f32[128,2048]{1,0:T(8,128)S(1)}) fusion(bf16[128,1024]{0,1:T(8,128)(2,1)S(1)} %bitcast.142, bf16[1024,2048]{1,0:T(8,128)(2,1)} %param.52, bf16[128,2048]{1,0:T(8,128)(2,1)S(1)} %copy-done.3), kind=kOutput, calls=%fused_computation.75 | convolution fusion | flops 537919360 | bytes 6029824 | tf_op jit(solution)/shard_map/dot_general | solution.py:172
  60.2 6.2 %collective-permute-done.24 = bf16[1,64,2048]{2,1,0:T(8,128)(2,1)S(1)} collective-permute-done((bf16[1,64,2048]{2,1,0:T(8,128)(2,1)S(1)}, bf16[1,64,2048]{2,1,0:T(8,128)(2,1)S(1)}, u32[]{:S(2)}, u32[]{:S(2)}) %collective-permute-start.24) | collective-permute-done | bytes 262176 | tf_op jit(solution)/shard_map/ppermute | solution.py:238
  70.1 1.5 reshape.159
  72.0 2.2 %slice_add_fusion = f32[1024,2,1]{2,1,0:T(2,128)S(1)} fusion(f32[1024,2,3]{2,1,0:T(2,128)S(1)} %reshape.159), kind=kLoop, calls=%fused_computation.66 | loop fusion | flops 4096 | bytes 32768 | tf_op jit(solution)/shard_map/add | solution.py:161
  74.7 6.5 %collective-permute-done.25 = bf16[2,64,2048]{2,1,0:T(8,128)(2,1)} collective-permute-done((bf16[2,64,2048]{2,1,0:T(8,128)(2,1)}, bf16[2,64,2048]{2,1,0:T(8,128)(2,1)}, u32[]{:S(2)}, u32[]{:S(2)}) %collective-permute-start.25) | collective-permute-done | bytes 524320 | tf_op jit(solution)/shard_map/ppermute | solution.py:238
  82.5 2.1 %collective-permute-done.26 = bf16[2,64,2048]{2,1,0:T(8,128)(2,1)} collective-permute-done((bf16[2,64,2048]{2,1,0:T(8,128)(2,1)}, bf16[2,64,2048]{2,1,0:T(8,128)(2,1)}, u32[]{:S(2)}, u32[]{:S(2)}) %collective-permute-start.26) | collective-permute-done | bytes 524320 | tf_op jit(solution)/shard_map/ppermute | solution.py:238
  84.6 2.3 %pad_maximum_fusion.4 = bf16[4,64,2048]{2,1,0:T(8,128)(2,1)} fusion(bf16[2,64,2048]{2,1,0:T(8,128)(2,1)} %collective-permute-done.26, bf16[2,64,2048]{2,1,0:T(8,128)(2,1)} %pad_maximum_fusion.6), kind=kLoop, calls=%fused_computation.69 | loop fusion | flops 524288 | bytes 2097152 | tf_op jit(solution)/shard_map/concatenate | solution.py:245
  89.7 1.4 pad_maximum_fusion
  91.4 1.9 %pad_maximum_fusion.1 = bf16[8,64,2048]{2,1,0:T(8,128)(2,1)S(1)} fusion(bf16[4,64,2048]{2,1,0:T(8,128)(2,1)} %collective-permute-done.28, bf16[4,64,2048]{2,1,0:T(8,128)(2,1)} %pad_maximum_fusion.4), kind=kLoop, calls=%fused_computation.19 | loop fusion | flops 1048576 | bytes 4194304 | tf_op jit(solution)/shard_map/concatenate | solution.py:245
  99.9 1.3 fusion.50
  101.2 1.3 fusion.56
  102.5 1.3 fusion.53
  103.9 1.3 fusion.59
  107.3 1.4 multiply_add_fusion.1
  110.3 1.4 multiply_add_fusion
  112.4 1.4 copy-done
  113.7 1.6 slice-done.1
  118.5 13.1 %collective-permute-done.32 = bf16[2,64,2048]{2,1,0:T(8,128)(2,1)S(1)} collective-permute-done((bf16[2,64,2048]{2,1,0:T(8,128)(2,1)S(1)}, bf16[2,64,2048]{2,1,0:T(8,128)(2,1)S(1)}, u32[]{:S(2)}, u32[]{:S(2)}) %collective-permute-start.32) | collective-permute-done | bytes 524320 | tf_op jit(solution)/shard_map/ppermute | solution.py:238
  134.8 1.8 %collective-permute-start.33 = (bf16[1,64,2048]{2,1,0:T(8,128)(2,1)S(1)}, bf16[1,64,2048]{2,1,0:T(8,128)(2,1)S(1)}, u32[]{:S(2)}, u32[]{:S(2)}) collective-permute-start(bf16[1,64,2048]{2,1,0:T(8,128)(2,1)S(1)} %slice.268), channel_id=1, source_target_pairs={{0,4},{1,5},{2,6},{3,7},{4,0},{5,1},{6,2},{7,3},{8,12},{9,13},{10,... | collective-permute-start | bytes 786440 | tf_op jit(solution)/shard_map/ppermute | solution.py:238
  136.6 4.0 %collective-permute-done.34 = bf16[1,64,2048]{2,1,0:T(8,128)(2,1)S(1)} collective-permute-done((bf16[1,64,2048]{2,1,0:T(8,128)(2,1)}, bf16[1,64,2048]{2,1,0:T(8,128)(2,1)S(1)}, u32[]{:S(2)}, u32[]{:S(2)}) %collective-permute-start.34) | collective-permute-done | bytes 262176 | tf_op jit(solution)/shard_map/ppermute | solution.py:238
  140.7 1.7 %collective-permute-done.33 = bf16[1,64,2048]{2,1,0:T(8,128)(2,1)S(1)} collective-permute-done((bf16[1,64,2048]{2,1,0:T(8,128)(2,1)S(1)}, bf16[1,64,2048]{2,1,0:T(8,128)(2,1)S(1)}, u32[]{:S(2)}, u32[]{:S(2)}) %collective-permute-start.33) | collective-permute-done | bytes 262176 | tf_op jit(solution)/shard_map/ppermute | solution.py:238
  142.6 16.1 %conditional.1 = (bf16[128,2048]{1,0:T(8,128)(2,1)S(1)}) conditional(s32[]{:T(128)} %clamp.3, bf16[128,2048]{1,0:T(8,128)(2,1)S(1)} %fusion.65, bf16[128,2048]{1,0:T(8,128)(2,1)S(1)} %fusion.65, bf16[128,2048]{1,0:T(8,128)(2,1)S(1)} %fusion.65, bf16[128,2048]{1,0:T(8,128)(2,1)S(1)} %fusion.65, ...), branch_computations={%region_8.10_spmd, %region_9.11_spmd, %region_10.12_spmd, %region_... | conditional | bytes 3145776 | solution.py:281
  142.6 4.5 %collective-permute-start.14 = (bf16[128,2048]{1,0:T(8,128)(2,1)S(1)}, bf16[128,2048]{1,0:T(8,128)(2,1)S(1)}, u32[]{:S(2)}, u32[]{:S(2)}) collective-permute-start(bf16[128,2048]{1,0:T(8,128)(2,1)S(1)} %param.17), channel_id=1, source_target_pairs={{0,16},{8,8},{16,24},{24,0},{1,17},{9,9},{17,25},{25,1},{2,18},{10... | collective-permute-start | bytes 1572872 | tf_op jit(solution)/shard_map/cond/branch_15_fun/ppermute | solution.py:279
  147.1 11.5 %collective-permute-done.14 = bf16[128,2048]{1,0:T(8,128)(2,1)S(1)} collective-permute-done((bf16[128,2048]{1,0:T(8,128)(2,1)S(1)}, bf16[128,2048]{1,0:T(8,128)(2,1)S(1)}, u32[]{:S(2)}, u32[]{:S(2)}) %collective-permute-start.14) | collective-permute-done | bytes 524320 | tf_op jit(solution)/shard_map/cond/branch_15_fun/ppermute | solution.py:279
  (117 shorter events, 39.6 us)
Async XLA Ops:
  0.0 5.8 %copy-start.5 = (bf16[192,1024]{1,0:T(8,128)(2,1)S(1)}, bf16[192,1024]{1,0:T(8,128)(2,1)}, u32[]{:S(2)}) copy-start(bf16[192,1024]{1,0:T(8,128)(2,1)} %param.48) | copy-start | bytes 1179652
  0.0 6.0 %copy-start.6 = (bf16[192,1024]{1,0:T(8,128)(2,1)S(1)}, bf16[192,1024]{1,0:T(8,128)(2,1)}, u32[]{:S(2)}) copy-start(bf16[192,1024]{1,0:T(8,128)(2,1)} %param.49) | copy-start | bytes 1179652
  8.2 7.5 %copy-start.11 = (s32[4]{0:T(128)S(1)}, s32[4]{0:T(128)}, u32[]{:S(2)}) copy-start(s32[4]{0:T(128)} %param.51) | copy-start | bytes 52
  8.2 8.1 %copy-start.15 = (s32[4]{0:T(128)S(1)}, s32[4]{0:T(128)}, u32[]{:S(2)}) copy-start(s32[4]{0:T(128)} %param.50) | copy-start | bytes 52
  10.5 26.4 %all-to-all-start = ((bf16[774,8,128]{2,0,1:T(8,128)(2,1)}), bf16[774,8,128]{2,0,1:T(8,128)(2,1)S(1)}, u32[]{:S(2)}, u32[]{:S(2)}) async-start(bf16[774,8,128]{2,0,1:T(8,128)(2,1)} %copy.110), calls=%async_computation | async-start | bytes 3178496 | tf_op jit(solution)/shard_map/all_to_all | solution.py:69
  36.9 2.0 %copy-start.2 = (bf16[774,8,128]{2,0,1:T(8,128)(2,1)}, bf16[774,8,128]{2,0,1:T(8,128)(2,1)S(1)}, u32[]{:S(2)}) copy-start(bf16[774,8,128]{2,0,1:T(8,128)(2,1)S(1)} %all-to-all-done) | copy-start | bytes 4755460
  41.6 14.1 %copy-start.3 = (bf16[128,2048]{1,0:T(8,128)(2,1)S(1)}, bf16[128,2048]{1,0:T(8,128)(2,1)}, u32[]{:S(2)}) copy-start(bf16[128,2048]{1,0:T(8,128)(2,1)} %param.44) | copy-start | bytes 1572868
  45.4 10.3 %all-to-all-start.1 = ((bf16[8,128,128]{1,2,0:T(8,128)(2,1)}), bf16[8,128,128]{1,2,0:T(8,128)(2,1)S(1)}, u32[]{:S(2)}, u32[]{:S(2)}) async-start(bf16[8,128,128]{1,2,0:T(8,128)(2,1)} %copy.111), calls=%async_computation.1 | async-start | bytes 524288 | tf_op jit(solution)/shard_map/all_to_all | solution.py:100
  55.7 3.1 %copy-start.7 = (f32[2048]{0:T(1024)S(1)}, f32[2048]{0:T(1024)}, u32[]{:S(2)}) copy-start(f32[2048]{0:T(1024)} %param.53) | copy-start | bytes 24580
  58.7 0.9 copy-start.9
  58.7 0.9 copy-start.10
  58.9 7.5 %collective-permute-start.24 = (bf16[1,64,2048]{2,1,0:T(8,128)(2,1)S(1)}, bf16[1,64,2048]{2,1,0:T(8,128)(2,1)S(1)}, u32[]{:S(2)}, u32[]{:S(2)}) collective-permute-start(bf16[1,64,2048]{2,1,0:T(8,128)(2,1)S(1)} %get-tuple-element.86), channel_id=1, source_target_pairs={{0,2},{1,3},{2,0},{3,1},{4,6},{5,7},{6,4},{7,5},{8,10},{9,11},{10,... | collective-permute-start | bytes 786440 | tf_op jit(solution)/shard_map/ppermute | solution.py:238
  59.6 7.9 %collective-permute-start.23 = (bf16[1,64,2048]{2,1,0:T(8,128)(2,1)S(1)}, bf16[1,64,2048]{2,1,0:T(8,128)(2,1)S(1)}, u32[]{:S(2)}, u32[]{:S(2)}) collective-permute-start(bf16[1,64,2048]{2,1,0:T(8,128)(2,1)S(1)} %get-tuple-element.87), channel_id=1, source_target_pairs={{0,4},{1,5},{2,6},{3,7},{4,0},{5,1},{6,2},{7,3},{8,12},{9,13},{10,... | collective-permute-start | bytes 786440 | tf_op jit(solution)/shard_map/ppermute | solution.py:238
  68.3 12.9 %collective-permute-start.25 = (bf16[2,64,2048]{2,1,0:T(8,128)(2,1)}, bf16[2,64,2048]{2,1,0:T(8,128)(2,1)}, u32[]{:S(2)}, u32[]{:S(2)}) collective-permute-start(bf16[2,64,2048]{2,1,0:T(8,128)(2,1)} %pad_maximum_fusion.5), channel_id=1, source_target_pairs={{0,2},{1,3},{2,0},{3,1},{4,6},{5,7},{6,4},{7,5},{8,10},{9,11},{10,... | collective-permute-start | bytes 1572872 | tf_op jit(solution)/shard_map/ppermute | solution.py:238
  71.6 13.0 %collective-permute-start.26 = (bf16[2,64,2048]{2,1,0:T(8,128)(2,1)}, bf16[2,64,2048]{2,1,0:T(8,128)(2,1)}, u32[]{:S(2)}, u32[]{:S(2)}) collective-permute-start(bf16[2,64,2048]{2,1,0:T(8,128)(2,1)} %pad_maximum_fusion.6), channel_id=1, source_target_pairs={{0,4},{1,5},{2,6},{3,7},{4,0},{5,1},{6,2},{7,3},{8,12},{9,13},{10,... | collective-permute-start | bytes 1572872 | tf_op jit(solution)/shard_map/ppermute | solution.py:238
  86.9 2.8 %collective-permute-start.27 = (bf16[4,64,2048]{2,1,0:T(8,128)(2,1)S(1)}, bf16[4,64,2048]{2,1,0:T(8,128)(2,1)}, u32[]{:S(2)}, u32[]{:S(2)}) collective-permute-start(bf16[4,64,2048]{2,1,0:T(8,128)(2,1)S(1)} %pad_maximum_fusion.3), channel_id=1, source_target_pairs={{0,1},{1,0},{2,3},{3,2},{4,5},{5,4},{6,7},{7,6},{8,9},{9,8},{10,11... | collective-permute-start | bytes 3145736 | tf_op jit(solution)/shard_map/ppermute | solution.py:238
  87.6 3.8 %collective-permute-start.28 = (bf16[4,64,2048]{2,1,0:T(8,128)(2,1)}, bf16[4,64,2048]{2,1,0:T(8,128)(2,1)}, u32[]{:S(2)}, u32[]{:S(2)}) collective-permute-start(bf16[4,64,2048]{2,1,0:T(8,128)(2,1)} %pad_maximum_fusion.4), channel_id=1, source_target_pairs={{0,1},{1,0},{2,3},{3,2},{4,5},{5,4},{6,7},{7,6},{8,9},{9,8},{10,11... | collective-permute-start | bytes 3145736 | tf_op jit(solution)/shard_map/ppermute | solution.py:238
  91.1 2.8 %copy-start.12 = (bf16[2,2048,512]{2,1,0:T(8,128)(2,1)S(1)}, bf16[2,2048,512]{2,1,0:T(8,128)(2,1)}, u32[]{:S(2)}) copy-start(bf16[2,2048,512]{2,1,0:T(8,128)(2,1)} %param.56) | copy-start | bytes 12582916
  97.7 2.2 %copy-start.13 = (bf16[2,2048,512]{2,1,0:T(8,128)(2,1)S(1)}, bf16[2,2048,512]{2,1,0:T(8,128)(2,1)}, u32[]{:S(2)}) copy-start(bf16[2,2048,512]{2,1,0:T(8,128)(2,1)} %param.57) | copy-start | bytes 12582916
  103.9 2.2 %copy-start.14 = (bf16[2,512,2048]{2,1,0:T(8,128)(2,1)S(1)}, bf16[2,512,2048]{2,1,0:T(8,128)(2,1)}, u32[]{:S(2)}) copy-start(bf16[2,512,2048]{2,1,0:T(8,128)(2,1)} %param.58) | copy-start | bytes 12582916
  108.7 3.7 %copy-start.1 = (f32[512,2048]{1,0:T(8,128)}, f32[512,2048]{1,0:T(8,128)S(1)}, u32[]{:S(2)}) copy-start(f32[512,2048]{1,0:T(8,128)S(1)} %multiply_add_fusion.1) | copy-start | bytes 12582916
  108.9 4.9 %collective-permute-start.29 = (bf16[4,64,2048]{2,1,0:T(8,128)(2,1)S(1)}, bf16[4,64,2048]{2,1,0:T(8,128)(2,1)S(1)}, u32[]{:S(2)}, u32[]{:S(2)}) collective-permute-start(bf16[4,64,2048]{2,1,0:T(8,128)(2,1)S(1)} %bitcast.143), channel_id=1, source_target_pairs={{0,1},{1,0},{2,3},{3,2},{4,5},{5,4},{6,7},{7,6},{8,9},{9,8},{10,11... | collective-permute-start | bytes 3145736 | tf_op jit(solution)/shard_map/ppermute | solution.py:238
  111.8 2.0 %copy-start = (f32[512,2048]{1,0:T(8,128)}, f32[512,2048]{1,0:T(8,128)S(1)}, u32[]{:S(2)}) copy-start(f32[512,2048]{1,0:T(8,128)S(1)} %multiply_add_fusion) | copy-start | bytes 12582916
  111.9 3.9 %collective-permute-start.30 = (bf16[4,64,2048]{2,1,0:T(8,128)(2,1)S(1)}, bf16[4,64,2048]{2,1,0:T(8,128)(2,1)S(1)}, u32[]{:S(2)}, u32[]{:S(2)}) collective-permute-start(bf16[4,64,2048]{2,1,0:T(8,128)(2,1)S(1)} %bitcast.144), channel_id=1, source_target_pairs={{0,1},{1,0},{2,3},{3,2},{4,5},{5,4},{6,7},{7,6},{8,9},{9,8},{10,11... | collective-permute-start | bytes 3145736 | tf_op jit(solution)/shard_map/ppermute | solution.py:238
  113.7 1.6 slice-start.1
  115.3 1.6 slice-start
  117.3 14.3 %collective-permute-start.32 = (bf16[2,64,2048]{2,1,0:T(8,128)(2,1)S(1)}, bf16[2,64,2048]{2,1,0:T(8,128)(2,1)S(1)}, u32[]{:S(2)}, u32[]{:S(2)}) collective-permute-start(bf16[2,64,2048]{2,1,0:T(8,128)(2,1)S(1)} %slice.265), channel_id=1, source_target_pairs={{0,4},{1,5},{2,6},{3,7},{4,0},{5,1},{6,2},{7,3},{8,12},{9,13},{10,... | collective-permute-start | bytes 1572872 | tf_op jit(solution)/shard_map/ppermute | solution.py:238
  117.8 15.6 %copy-start.8 = (s32[24,4]{0,1:T(4,128)S(1)}, s32[24,4]{0,1:T(4,128)}, u32[]{:S(2)}) copy-start(s32[24,4]{0,1:T(4,128)} %constant.76.clone) | copy-start | bytes 1156
  117.8 14.0 %collective-permute-start.31 = (bf16[2,64,2048]{2,1,0:T(8,128)(2,1)S(1)}, bf16[2,64,2048]{2,1,0:T(8,128)(2,1)S(1)}, u32[]{:S(2)}, u32[]{:S(2)}) collective-permute-start(bf16[2,64,2048]{2,1,0:T(8,128)(2,1)S(1)} %slice.266), channel_id=1, source_target_pairs={{0,2},{1,3},{2,0},{3,1},{4,6},{5,7},{6,4},{7,5},{8,10},{9,11},{10,... | collective-permute-start | bytes 1572872 | tf_op jit(solution)/shard_map/ppermute | solution.py:238
  132.7 7.9 %collective-permute-start.34 = (bf16[1,64,2048]{2,1,0:T(8,128)(2,1)}, bf16[1,64,2048]{2,1,0:T(8,128)(2,1)S(1)}, u32[]{:S(2)}, u32[]{:S(2)}) collective-permute-start(bf16[1,64,2048]{2,1,0:T(8,128)(2,1)} %slice.267), channel_id=1, source_target_pairs={{0,2},{1,3},{2,0},{3,1},{4,6},{5,7},{6,4},{7,5},{8,10},{9,11},{10,... | collective-permute-start | bytes 786440 | tf_op jit(solution)/shard_map/ppermute | solution.py:238
  134.8 7.5 %collective-permute-start.33 = (bf16[1,64,2048]{2,1,0:T(8,128)(2,1)S(1)}, bf16[1,64,2048]{2,1,0:T(8,128)(2,1)S(1)}, u32[]{:S(2)}, u32[]{:S(2)}) collective-permute-start(bf16[1,64,2048]{2,1,0:T(8,128)(2,1)S(1)} %slice.268), channel_id=1, source_target_pairs={{0,4},{1,5},{2,6},{3,7},{4,0},{5,1},{6,2},{7,3},{8,12},{9,13},{10,... | collective-permute-start | bytes 786440 | tf_op jit(solution)/shard_map/ppermute | solution.py:238
  142.6 16.0 %collective-permute-start.14 = (bf16[128,2048]{1,0:T(8,128)(2,1)S(1)}, bf16[128,2048]{1,0:T(8,128)(2,1)S(1)}, u32[]{:S(2)}, u32[]{:S(2)}) collective-permute-start(bf16[128,2048]{1,0:T(8,128)(2,1)S(1)} %param.17), channel_id=1, source_target_pairs={{0,16},{8,8},{16,24},{24,0},{1,17},{9,9},{17,25},{25,1},{2,18},{10... | collective-permute-start | bytes 1572872 | tf_op jit(solution)/shard_map/cond/branch_15_fun/ppermute | solution.py:279
  (1 other events, 0.8 us)
where the time goes:
time: 160 us; the launch traced here: 159 us
  waiting for transfers between devices  71.6 us (45%)
  matrix products  23.4 us (15%)
  local copies, waits for them, and re-layouts  21.3 us (13%)
  other arithmetic  21.1 us (13%)
  starting transfers between devices  20.7 us (13%)
    ppermute x12, waiting for transfers between devices, swap(): return lax.ppermute(rows, 'ctx', [(c, c ^ mask) for c in range(ctx_count)])  34.8 us
    all_to_all x1, waiting for transfers between devices, attend_by_head(): got = lax.all_to_all(packed, 'ctx', split_axis=1, concat_axis=0, tiled=True)  18.6 us
    ppermute x1, waiting for transfers between devices, mover(): return lambda rows: lax.ppermute(rows, 'req', pairs)  11.5 us
    concatenate x6, other arithmetic, gather_xor(): jnp.concatenate([held, swap(held, 1 << order[step], ctx_count)], 0)  8.55 us
    unnamed x38, local copies, waits for them, and re-layouts  8.45 us
    ppermute x12, starting transfers between devices, swap(): return lax.ppermute(rows, 'ctx', [(c, c ^ mask) for c in range(ctx_count)])  7.42 us
    all_to_all x1, waiting for transfers between devices, attend_by_head(): lax.all_to_all(head_out, 'ctx', split_axis=0, concat_axis=0, tiled=True)  6.69 us
    dot_general x4, matrix products, experts_on(): up_val = jnp.dot(rows, up_proj[j], preferred_element_type=jnp.float32)  5.33 us
  transfers between devices with their start and end apart: 15, of which 13 were waited for; matrix products, arithmetic and copies ran while one was open for 11% of the time, Pallas kernels for 0%

commit v1 on v0

--- a/solution.py
+++ b/solution.py
@@ -189,24 +189,35 @@
             moe = term if moe is None else moe + term
         return moe
 
-    if ctx_count & (ctx_count - 1) == 0 and ctx_count > 1 and token_count % 2 == 0:
+    if ctx_count & (ctx_count - 1) == 0 and ctx_count > 1 and token_count % 4 == 0:
         me = lax.axis_index("ctx")
-        half_rows = token_count // 2
+        stream_rows = token_count // 4
         gate_blocks = local_gates.reshape(ctx_count, token_count, local_experts)
         orders = xor_orders(ctx_count)
-        helds = gather_xor(
-            [normed[h * half_rows : (h + 1) * half_rows] for h in range(2)], orders, ctx_count
-        )
-        parts = []
-        for half, order in enumerate(orders):
-            sources = jnp.array(relative_masks(order), jnp.int32) ^ me
-            gates = jnp.take(
-                gate_blocks[:, half * half_rows : (half + 1) * half_rows], sources, axis=0
-            ).reshape(ctx_count * half_rows, local_experts)
-            part = experts_on(helds[half].reshape(ctx_count * half_rows, feature_width), gates)
-            parts.append(part.reshape(ctx_count, half_rows, feature_width))
-        moe_halves = reduce_xor(parts, orders, ctx_count)
-        moe_rows = jnp.concatenate(moe_halves, 0)
+        moe_pieces = []
+        earlier = None
+        for group in range(2):
+            firsts = [(2 * group + s) * stream_rows for s in range(2)]
+            inputs = [normed[f : f + stream_rows] for f in firsts]
+            if earlier is not None:
+                inputs, _ = lax.optimization_barrier((inputs, earlier))
+            helds = gather_xor(inputs, orders, ctx_count)
+            earlier = helds
+            gates = []
+            for first, order in zip(firsts, orders):
+                sources = jnp.array(relative_masks(order), jnp.int32) ^ me
+                gates.append(
+                    jnp.take(
+                        gate_blocks[:, first : first + stream_rows], sources, axis=0
+                    ).reshape(ctx_count * stream_rows, local_experts)
+                )
+            rows = jnp.concatenate(
+                [held.reshape(ctx_count * stream_rows, feature_width) for held in helds], 0
+            )
+            part = experts_on(rows, jnp.concatenate(gates, 0))
+            part = part.reshape(2, ctx_count, stream_rows, feature_width)
+            moe_pieces.extend(reduce_xor([part[0], part[1]], orders, ctx_count))
+        moe_rows = jnp.concatenate(moe_pieces, 0)
     else:
         normed_all = lax.all_gather(normed, "ctx", axis=0, tiled=True)
         moe = experts_on(normed_all, local_gates)

time: 160 us -> 157 us (0.981)
  the two profiles are of different devices: /device:TPU:0 before, /device:TPU:8 now
where the time goes in v1:
time: 157 us
  waiting for transfers between devices  67 us (43%)
  starting transfers between devices  30.2 us (19%)
  matrix products  23.9 us (15%)
  local copies, waits for them, and re-layouts  19.8 us (13%)
  other arithmetic  14.3 us (9%)
    ppermute x24, waiting for transfers between devices, swap(): return lax.ppermute(rows, 'ctx', [(c, c ^ mask) for c in range(ctx_count)])  38.4 us
    ppermute x24, starting transfers between devices, swap(): return lax.ppermute(rows, 'ctx', [(c, c ^ mask) for c in range(ctx_count)])  18.4 us
    all_to_all x1, waiting for transfers between devices, attend_by_head(): got = lax.all_to_all(packed, 'ctx', split_axis=1, concat_axis=0, tiled=True)  15 us
    ppermute x1, waiting for transfers between devices, mover(): return lambda rows: lax.ppermute(rows, 'req', pairs)  10 us
    unnamed x38, local copies, waits for them, and re-layouts  7.5 us
    dot_general x4, matrix products, experts_on(): up_val = jnp.dot(rows, up_proj[j], preferred_element_type=jnp.float32)  5.6 us
    dot_general x4, matrix products, experts_on(): jnp.dot(activated, down_proj[j], preferred_element_type=jnp.float32)  5.45 us
    dot_general x4, matrix products, experts_on(): gate_val = jnp.dot(rows, gate_proj[j], preferred_element_type=jnp.float32)  5.02 us
  transfers between devices with their start and end apart: 27, of which 18 were waited for; matrix products, arithmetic and copies ran while one was open for 16% of the time, Pallas kernels for 0%

profile of v1, /device:TPU:8, one launch (start us, length us, event | category | flops | bytes accessed | tf_op | source)
XLA Modules:
  0.0 156.6 jit_solution(8312119683572423262)
XLA Ops:
  10.1 2.3 %copy.122 = bf16[774,8,128]{2,0,1:T(8,128)(2,1)} copy(bf16[774,8,128]{0,2,1:T(8,128)(2,1)S(1)} %pad_maximum_fusion.2) | data formatting | bytes 3170304 | tf_op jit(solution)/shard_map/concatenate | solution.py:67
  12.4 3.7 %all-to-all-start = ((bf16[774,8,128]{2,0,1:T(8,128)(2,1)}), bf16[774,8,128]{2,0,1:T(8,128)(2,1)S(1)}, u32[]{:S(2)}, u32[]{:S(2)}) async-start(bf16[774,8,128]{2,0,1:T(8,128)(2,1)} %copy.122), calls=%async_computation | async-start | bytes 3178496 | tf_op jit(solution)/shard_map/all_to_all | solution.py:69
  22.4 15.0 %all-to-all-done = bf16[774,8,128]{2,0,1:T(8,128)(2,1)S(1)} async-done(((bf16[774,8,128]{2,0,1:T(8,128)(2,1)}), bf16[774,8,128]{2,0,1:T(8,128)(2,1)S(1)}, u32[]{:S(2)}, u32[]{:S(2)}) %all-to-all-start) | async-done | bytes 1585184 | tf_op jit(solution)/shard_map/all_to_all | solution.py:69
  38.4 1.5 reshape.189
  39.9 2.2 %slice_add_fusion = f32[1024,2,1]{2,1,0:T(2,128)S(1)} fusion(f32[1024,2,3]{2,1,0:T(2,128)S(1)} %reshape.189), kind=kLoop, calls=%fused_computation.62 | loop fusion | flops 4096 | bytes 32768 | tf_op jit(solution)/shard_map/add | solution.py:161
  42.6 1.8 %fusion = (f32[1024]{0:T(1024)S(1)}, f32[1024,2560]{1,0:T(8,128)S(1)}) fusion(pred[2560]{0:T(1024)(128)(4,1)S(1)} %copy-done.4, bf16[1024,128]{1,0:T(8,128)(2,1)S(1)} %bitcast.144, bf16[2560,128]{1,0:T(8,128)(2,1)S(1)} %bitcast.143), kind=kOutput, calls=%fused_computation.6 | convolution fusion | flops 678951936 | bytes 11409920 | tf_op jit(solution)/shard_map/thd,phd->htp/dot_general | solution.py:85
  44.4 2.7 %fusion.1 = f32[1024]{0:T(1024)S(1)} fusion(f32[1024,2560]{1,0:T(8,128)S(1)} %get-tuple-element.142, f32[1024]{0:T(1024)S(1)} %get-tuple-element.141, pred[2560]{0:T(1024)(128)(4,1)S(1)} %copy-done.4), kind=kLoop, calls=%fused_computation.7 | loop fusion | flops 13106176 | bytes 10496512 | tf_op jit(solution)/shard_map/reduce_sum | solution.py:91
  47.1 3.0 %fusion.72 = bf16[16,8,8,128]{3,1,2,0:T(8,128)(2,1)S(1)} fusion(bf16[2560,128]{1,0:T(8,128)(2,1)S(1)} %bitcast.168, f32[1024,2560]{1,0:T(8,128)S(1)} %get-tuple-element.142, f32[1024]{0:T(1024)S(1)} %get-tuple-element.141, pred[2560]{0:T(1024)(128)(4,1)S(1)} %copy-done.4, f32[1024]{0:T(1024)S(1)} %fusion.1), kind=kOutput, calls=%fused_computation.78 | convolution fusion | flops 684457984 | bytes 11414016 | tf_op jit(solution)/shard_map/htp,phd->thd/dot_general | solution.py:92
  50.9 3.6 %all-to-all-start.1 = ((bf16[8,128,128]{1,2,0:T(8,128)(2,1)}), bf16[8,128,128]{1,2,0:T(8,128)(2,1)S(1)}, u32[]{:S(2)}, u32[]{:S(2)}) async-start(bf16[8,128,128]{1,2,0:T(8,128)(2,1)} %copy.123), calls=%async_computation.1 | async-start | bytes 524288 | tf_op jit(solution)/shard_map/all_to_all | solution.py:100
  57.6 3.6 %all-to-all-done.1 = bf16[8,128,128]{1,2,0:T(8,128)(2,1)S(1)} async-done(((bf16[8,128,128]{1,2,0:T(8,128)(2,1)}), bf16[8,128,128]{1,2,0:T(8,128)(2,1)S(1)}, u32[]{:S(2)}, u32[]{:S(2)}) %all-to-all-start.1) | async-done | bytes 262176 | tf_op jit(solution)/shard_map/all_to_all | solution.py:100
  61.2 3.0 %multiply_reduce_fusion = (f32[128]{0:T(128)S(1)}, f32[128,2048]{1,0:T(8,128)S(1)}) fusion(bf16[128,1024]{0,1:T(8,128)(2,1)S(1)} %bitcast.147, bf16[1024,2048]{1,0:T(8,128)(2,1)} %param.54, bf16[128,2048]{1,0:T(8,128)(2,1)S(1)} %copy-done.2), kind=kOutput, calls=%fused_computation.75 | convolution fusion | flops 537919360 | bytes 6029824 | tf_op jit(solution)/shard_map/dot_general | solution.py:172
  65.8 3.7 %collective-permute-done.24 = bf16[1,32,2048]{2,1,0:T(8,128)(2,1)S(1)} collective-permute-done((bf16[1,32,2048]{2,1,0:T(8,128)(2,1)S(1)}, bf16[1,32,2048]{2,1,0:T(8,128)(2,1)S(1)}, u32[]{:S(2)}, u32[]{:S(2)}) %collective-permute-start.24) | collective-permute-done | bytes 131104 | tf_op jit(solution)/shard_map/ppermute | solution.py:249
  70.3 1.5 collective-permute-start.25
  72.6 4.8 %collective-permute-done.25 = bf16[2,32,2048]{2,1,0:T(8,128)(2,1)S(1)} collective-permute-done((bf16[2,32,2048]{2,1,0:T(8,128)(2,1)S(1)}, bf16[2,32,2048]{2,1,0:T(8,128)(2,1)S(1)}, u32[]{:S(2)}, u32[]{:S(2)}) %collective-permute-start.25) | collective-permute-done | bytes 262176 | tf_op jit(solution)/shard_map/ppermute | solution.py:249
  78.9 1.4 collective-permute-done.27
  86.4 1.3 fusion.59
  89.9 1.4 fusion.101
  93.6 1.5 collective-permute-start.38
  96.2 4.4 %collective-permute-done.37 = bf16[2,32,2048]{2,1,0:T(8,128)(2,1)S(1)} collective-permute-done((bf16[2,32,2048]{2,1,0:T(8,128)(2,1)S(1)}, bf16[2,32,2048]{2,1,0:T(8,128)(2,1)S(1)}, u32[]{:S(2)}, u32[]{:S(2)}) %collective-permute-start.37) | collective-permute-done | bytes 262176 | tf_op jit(solution)/shard_map/ppermute | solution.py:249
  100.6 2.1 %collective-permute-done.38 = bf16[2,32,2048]{2,1,0:T(8,128)(2,1)S(1)} collective-permute-done((bf16[2,32,2048]{2,1,0:T(8,128)(2,1)S(1)}, bf16[2,32,2048]{2,1,0:T(8,128)(2,1)S(1)}, u32[]{:S(2)}, u32[]{:S(2)}) %collective-permute-start.38) | collective-permute-done | bytes 262176 | tf_op jit(solution)/shard_map/ppermute | solution.py:249
  104.3 2.9 %collective-permute-done.32 = bf16[2,32,2048]{2,1,0:T(8,128)(2,1)S(1)} collective-permute-done((bf16[2,32,2048]{2,1,0:T(8,128)(2,1)S(1)}, bf16[2,32,2048]{2,1,0:T(8,128)(2,1)S(1)}, u32[]{:S(2)}, u32[]{:S(2)}) %collective-permute-start.32) | collective-permute-done | bytes 262176 | tf_op jit(solution)/shard_map/ppermute | solution.py:249
  107.3 4.5 %collective-permute-done.31 = bf16[2,32,2048]{2,1,0:T(8,128)(2,1)S(1)} collective-permute-done((bf16[2,32,2048]{2,1,0:T(8,128)(2,1)S(1)}, bf16[2,32,2048]{2,1,0:T(8,128)(2,1)S(1)}, u32[]{:S(2)}, u32[]{:S(2)}) %collective-permute-start.31) | collective-permute-done | bytes 262176 | tf_op jit(solution)/shard_map/ppermute | solution.py:249
  112.7 1.7 %collective-permute-start.33 = (bf16[1,32,2048]{2,1,0:T(8,128)(2,1)S(1)}, bf16[1,32,2048]{2,1,0:T(8,128)(2,1)S(1)}, u32[]{:S(2)}, u32[]{:S(2)}) collective-permute-start(bf16[1,32,2048]{2,1,0:T(8,128)(2,1)S(1)} %slice.388), channel_id=1, source_target_pairs={{0,4},{1,5},{2,6},{3,7},{4,0},{5,1},{6,2},{7,3},{8,12},{9,13},{10,... | collective-permute-start | bytes 393224 | tf_op jit(solution)/shard_map/ppermute | solution.py:249
  118.5 1.6 %fusion.56 = bf16[512,512]{1,0:T(8,128)(2,1)S(1)} fusion(bf16[2,2048,512]{2,1,0:T(8,128)(2,1)S(1)} %copy-done.13, f32[512,512]{1,0:T(8,128)S(1)} %fusion.22, bf16[256,2048]{1,0:T(8,128)(2,1)S(1)} %bitcast.166, bf16[256,2048]{1,0:T(8,128)(2,1)S(1)} %bitcast.162), kind=kOutput, calls=%fused_computation.59 | convolution fusion | flops 1079508992 | bytes 5767168 | tf_op jit(solution)/shard_map/dot_general | solution.py:182
  121.4 1.4 fusion.100
  123.6 2.0 %collective-permute-done.42 = bf16[4,32,2048]{2,1,0:T(8,128)(2,1)S(1)} collective-permute-done((bf16[4,32,2048]{2,1,0:T(8,128)(2,1)S(1)}, bf16[4,32,2048]{2,1,0:T(8,128)(2,1)S(1)}, u32[]{:S(2)}, u32[]{:S(2)}) %collective-permute-start.42) | collective-permute-done | bytes 524320 | tf_op jit(solution)/shard_map/ppermute | solution.py:249
  127.7 6.6 %collective-permute-done.44 = bf16[2,32,2048]{2,1,0:T(8,128)(2,1)S(1)} collective-permute-done((bf16[2,32,2048]{2,1,0:T(8,128)(2,1)S(1)}, bf16[2,32,2048]{2,1,0:T(8,128)(2,1)S(1)}, u32[]{:S(2)}, u32[]{:S(2)}) %collective-permute-start.44) | collective-permute-done | bytes 262176 | tf_op jit(solution)/shard_map/ppermute | solution.py:249
  136.0 1.6 %collective-permute-start.45 = (bf16[1,32,2048]{2,1,0:T(8,128)(2,1)S(1)}, bf16[1,32,2048]{2,1,0:T(8,128)(2,1)S(1)}, u32[]{:S(2)}, u32[]{:S(2)}) collective-permute-start(bf16[1,32,2048]{2,1,0:T(8,128)(2,1)S(1)} %slice.386), channel_id=1, source_target_pairs={{0,4},{1,5},{2,6},{3,7},{4,0},{5,1},{6,2},{7,3},{8,12},{9,13},{10,... | collective-permute-start | bytes 393224 | tf_op jit(solution)/shard_map/ppermute | solution.py:249
  137.6 2.1 %collective-permute-done.46 = bf16[1,32,2048]{2,1,0:T(8,128)(2,1)S(1)} collective-permute-done((bf16[1,32,2048]{2,1,0:T(8,128)(2,1)S(1)}, bf16[1,32,2048]{2,1,0:T(8,128)(2,1)S(1)}, u32[]{:S(2)}, u32[]{:S(2)}) %collective-permute-start.46) | collective-permute-done | bytes 131104 | tf_op jit(solution)/shard_map/ppermute | solution.py:249
  141.2 14.6 %conditional.1 = (bf16[128,2048]{1,0:T(8,128)(2,1)S(1)}) conditional(s32[]{:T(128)} %clamp.3, bf16[128,2048]{1,0:T(8,128)(2,1)S(1)} %fusion.65, bf16[128,2048]{1,0:T(8,128)(2,1)S(1)} %fusion.65, bf16[128,2048]{1,0:T(8,128)(2,1)S(1)} %fusion.65, bf16[128,2048]{1,0:T(8,128)(2,1)S(1)} %fusion.65, ...), branch_computations={%region_8.10_spmd, %region_9.11_spmd, %region_10.12_spmd, %region_... | conditional | bytes 3145776 | solution.py:292
  141.3 4.5 %collective-permute-start.4 = (bf16[128,2048]{1,0:T(8,128)(2,1)S(1)}, bf16[128,2048]{1,0:T(8,128)(2,1)S(1)}, u32[]{:S(2)}, u32[]{:S(2)}) collective-permute-start(bf16[128,2048]{1,0:T(8,128)(2,1)S(1)} %param.7), channel_id=1, source_target_pairs={{0,0},{8,24},{16,16},{24,8},{1,1},{9,25},{17,17},{25,9},{2,2},{10,... | collective-permute-start | bytes 1572872 | tf_op jit(solution)/shard_map/cond/branch_5_fun/ppermute | solution.py:290
  145.8 10.0 %collective-permute-done.4 = bf16[128,2048]{1,0:T(8,128)(2,1)S(1)} collective-permute-done((bf16[128,2048]{1,0:T(8,128)(2,1)S(1)}, bf16[128,2048]{1,0:T(8,128)(2,1)S(1)}, u32[]{:S(2)}, u32[]{:S(2)}) %collective-permute-start.4) | collective-permute-done | bytes 524320 | tf_op jit(solution)/shard_map/cond/branch_5_fun/ppermute | solution.py:290
  (163 shorter events, 51.7 us)
Async XLA Ops:
  10.1 10.5 %copy-start.9 = (s32[8]{0:T(128)S(1)}, s32[8]{0:T(128)}, u32[]{:S(2)}) copy-start(s32[8]{0:T(128)} %constant.75.clone) | copy-start | bytes 100
  10.1 10.5 %copy-start.10 = (s32[8]{0:T(128)S(1)}, s32[8]{0:T(128)}, u32[]{:S(2)}) copy-start(s32[8]{0:T(128)} %constant.74.clone) | copy-start | bytes 100
  12.4 24.9 %all-to-all-start = ((bf16[774,8,128]{2,0,1:T(8,128)(2,1)}), bf16[774,8,128]{2,0,1:T(8,128)(2,1)S(1)}, u32[]{:S(2)}, u32[]{:S(2)}) async-start(bf16[774,8,128]{2,0,1:T(8,128)(2,1)} %copy.122), calls=%async_computation | async-start | bytes 3178496 | tf_op jit(solution)/shard_map/all_to_all | solution.py:69
  47.1 10.3 %copy-start.7 = (pred[8]{0:T(512)(128)(4,1)S(1)}, pred[8]{0:T(512)(128)(4,1)}, u32[]{:S(2)}) copy-start(pred[8]{0:T(512)(128)(4,1)} %get-tuple-element.149) | copy-start | bytes 28
  47.1 14.1 %copy-start.2 = (bf16[128,2048]{1,0:T(8,128)(2,1)S(1)}, bf16[128,2048]{1,0:T(8,128)(2,1)}, u32[]{:S(2)}) copy-start(bf16[128,2048]{1,0:T(8,128)(2,1)} %param.46) | copy-start | bytes 1572868
  50.2 14.1 %copy-start.5 = (f32[2048]{0:T(1024)S(1)}, f32[2048]{0:T(1024)}, u32[]{:S(2)}) copy-start(f32[2048]{0:T(1024)} %param.55) | copy-start | bytes 24580
  50.9 10.3 %all-to-all-start.1 = ((bf16[8,128,128]{1,2,0:T(8,128)(2,1)}), bf16[8,128,128]{1,2,0:T(8,128)(2,1)S(1)}, u32[]{:S(2)}, u32[]{:S(2)}) async-start(bf16[8,128,128]{1,2,0:T(8,128)(2,1)} %copy.123), calls=%async_computation.1 | async-start | bytes 524288 | tf_op jit(solution)/shard_map/all_to_all | solution.py:100
  64.5 5.0 %collective-permute-start.24 = (bf16[1,32,2048]{2,1,0:T(8,128)(2,1)S(1)}, bf16[1,32,2048]{2,1,0:T(8,128)(2,1)S(1)}, u32[]{:S(2)}, u32[]{:S(2)}) collective-permute-start(bf16[1,32,2048]{2,1,0:T(8,128)(2,1)S(1)} %get-tuple-element.122), channel_id=1, source_target_pairs={{0,2},{1,3},{2,0},{3,1},{4,6},{5,7},{6,4},{7,5},{8,10},{9,11},{10,... | collective-permute-start | bytes 393224 | tf_op jit(solution)/shard_map/ppermute | solution.py:249
  65.2 5.1 %collective-permute-start.23 = (bf16[1,32,2048]{2,1,0:T(8,128)(2,1)S(1)}, bf16[1,32,2048]{2,1,0:T(8,128)(2,1)S(1)}, u32[]{:S(2)}, u32[]{:S(2)}) collective-permute-start(bf16[1,32,2048]{2,1,0:T(8,128)(2,1)S(1)} %get-tuple-element.125), channel_id=1, source_target_pairs={{0,4},{1,5},{2,6},{3,7},{4,0},{5,1},{6,2},{7,3},{8,12},{9,13},{10,... | collective-permute-start | bytes 393224 | tf_op jit(solution)/shard_map/ppermute | solution.py:249
  70.3 7.0 %collective-permute-start.25 = (bf16[2,32,2048]{2,1,0:T(8,128)(2,1)S(1)}, bf16[2,32,2048]{2,1,0:T(8,128)(2,1)S(1)}, u32[]{:S(2)}, u32[]{:S(2)}) collective-permute-start(bf16[2,32,2048]{2,1,0:T(8,128)(2,1)S(1)} %pad_maximum_fusion.11), channel_id=1, source_target_pairs={{0,2},{1,3},{2,0},{3,1},{4,6},{5,7},{6,4},{7,5},{8,10},{9,11},{10,... | collective-permute-start | bytes 786440 | tf_op jit(solution)/shard_map/ppermute | solution.py:249
  71.9 6.4 %collective-permute-start.26 = (bf16[2,32,2048]{2,1,0:T(8,128)(2,1)S(1)}, bf16[2,32,2048]{2,1,0:T(8,128)(2,1)S(1)}, u32[]{:S(2)}, u32[]{:S(2)}) collective-permute-start(bf16[2,32,2048]{2,1,0:T(8,128)(2,1)S(1)} %pad_maximum_fusion.12), channel_id=1, source_target_pairs={{0,4},{1,5},{2,6},{3,7},{4,0},{5,1},{6,2},{7,3},{8,12},{9,13},{10,... | collective-permute-start | bytes 786440 | tf_op jit(solution)/shard_map/ppermute | solution.py:249
  78.3 2.0 %collective-permute-start.27 = (bf16[4,32,2048]{2,1,0:T(8,128)(2,1)S(1)}, bf16[4,32,2048]{2,1,0:T(8,128)(2,1)S(1)}, u32[]{:S(2)}, u32[]{:S(2)}) collective-permute-start(bf16[4,32,2048]{2,1,0:T(8,128)(2,1)S(1)} %pad_maximum_fusion.7), channel_id=1, source_target_pairs={{0,1},{1,0},{2,3},{3,2},{4,5},{5,4},{6,7},{7,6},{8,9},{9,8},{10,11... | collective-permute-start | bytes 1572872 | tf_op jit(solution)/shard_map/ppermute | solution.py:249
  78.4 2.6 %collective-permute-start.28 = (bf16[4,32,2048]{2,1,0:T(8,128)(2,1)S(1)}, bf16[4,32,2048]{2,1,0:T(8,128)(2,1)S(1)}, u32[]{:S(2)}, u32[]{:S(2)}) collective-permute-start(bf16[4,32,2048]{2,1,0:T(8,128)(2,1)S(1)} %pad_maximum_fusion.8), channel_id=1, source_target_pairs={{0,1},{1,0},{2,3},{3,2},{4,5},{5,4},{6,7},{7,6},{8,9},{9,8},{10,11... | collective-permute-start | bytes 1572872 | tf_op jit(solution)/shard_map/ppermute | solution.py:249
  83.7 8.4 %collective-permute-start.36 = (bf16[1,32,2048]{2,1,0:T(8,128)(2,1)S(1)}, bf16[1,32,2048]{2,1,0:T(8,128)(2,1)S(1)}, u32[]{:S(2)}, u32[]{:S(2)}) collective-permute-start(bf16[1,32,2048]{2,1,0:T(8,128)(2,1)S(1)} %bitcast.175), channel_id=1, source_target_pairs={{0,2},{1,3},{2,0},{3,1},{4,6},{5,7},{6,4},{7,5},{8,10},{9,11},{10,... | collective-permute-start | bytes 393224 | tf_op jit(solution)/shard_map/ppermute | solution.py:249
  84.7 7.5 %collective-permute-start.35 = (bf16[1,32,2048]{2,1,0:T(8,128)(2,1)S(1)}, bf16[1,32,2048]{2,1,0:T(8,128)(2,1)S(1)}, u32[]{:S(2)}, u32[]{:S(2)}) collective-permute-start(bf16[1,32,2048]{2,1,0:T(8,128)(2,1)S(1)} %bitcast.173), channel_id=1, source_target_pairs={{0,4},{1,5},{2,6},{3,7},{4,0},{5,1},{6,2},{7,3},{8,12},{9,13},{10,... | collective-permute-start | bytes 393224 | tf_op jit(solution)/shard_map/ppermute | solution.py:249
  91.4 3.8 %collective-permute-start.29 = (bf16[4,32,2048]{2,1,0:T(8,128)(2,1)S(1)}, bf16[4,32,2048]{2,1,0:T(8,128)(2,1)S(1)}, u32[]{:S(2)}, u32[]{:S(2)}) collective-permute-start(bf16[4,32,2048]{2,1,0:T(8,128)(2,1)S(1)} %bitcast.169), channel_id=1, source_target_pairs={{0,1},{1,0},{2,3},{3,2},{4,5},{5,4},{6,7},{7,6},{8,9},{9,8},{10,11... | collective-permute-start | bytes 1572872 | tf_op jit(solution)/shard_map/ppermute | solution.py:249
  91.5 3.6 %collective-permute-start.30 = (bf16[4,32,2048]{2,1,0:T(8,128)(2,1)S(1)}, bf16[4,32,2048]{2,1,0:T(8,128)(2,1)S(1)}, u32[]{:S(2)}, u32[]{:S(2)}) collective-permute-start(bf16[4,32,2048]{2,1,0:T(8,128)(2,1)S(1)} %bitcast.170), channel_id=1, source_target_pairs={{0,1},{1,0},{2,3},{3,2},{4,5},{5,4},{6,7},{7,6},{8,9},{9,8},{10,11... | collective-permute-start | bytes 1572872 | tf_op jit(solution)/shard_map/ppermute | solution.py:249
  92.2 8.4 %collective-permute-start.37 = (bf16[2,32,2048]{2,1,0:T(8,128)(2,1)S(1)}, bf16[2,32,2048]{2,1,0:T(8,128)(2,1)S(1)}, u32[]{:S(2)}, u32[]{:S(2)}) collective-permute-start(bf16[2,32,2048]{2,1,0:T(8,128)(2,1)S(1)} %pad_maximum_fusion.13), channel_id=1, source_target_pairs={{0,2},{1,3},{2,0},{3,1},{4,6},{5,7},{6,4},{7,5},{8,10},{9,11},{10,... | collective-permute-start | bytes 786440 | tf_op jit(solution)/shard_map/ppermute | solution.py:249
  93.6 9.2 %collective-permute-start.38 = (bf16[2,32,2048]{2,1,0:T(8,128)(2,1)S(1)}, bf16[2,32,2048]{2,1,0:T(8,128)(2,1)S(1)}, u32[]{:S(2)}, u32[]{:S(2)}) collective-permute-start(bf16[2,32,2048]{2,1,0:T(8,128)(2,1)S(1)} %pad_maximum_fusion.14), channel_id=1, source_target_pairs={{0,4},{1,5},{2,6},{3,7},{4,0},{5,1},{6,2},{7,3},{8,12},{9,13},{10,... | collective-permute-start | bytes 786440 | tf_op jit(solution)/shard_map/ppermute | solution.py:249
  95.4 11.8 %collective-permute-start.32 = (bf16[2,32,2048]{2,1,0:T(8,128)(2,1)S(1)}, bf16[2,32,2048]{2,1,0:T(8,128)(2,1)S(1)}, u32[]{:S(2)}, u32[]{:S(2)}) collective-permute-start(bf16[2,32,2048]{2,1,0:T(8,128)(2,1)S(1)} %slice.383), channel_id=1, source_target_pairs={{0,4},{1,5},{2,6},{3,7},{4,0},{5,1},{6,2},{7,3},{8,12},{9,13},{10,... | collective-permute-start | bytes 786440 | tf_op jit(solution)/shard_map/ppermute | solution.py:249
  102.8 11.6 %collective-permute-start.39 = (bf16[4,32,2048]{2,1,0:T(8,128)(2,1)S(1)}, bf16[4,32,2048]{2,1,0:T(8,128)(2,1)S(1)}, u32[]{:S(2)}, u32[]{:S(2)}) collective-permute-start(bf16[4,32,2048]{2,1,0:T(8,128)(2,1)S(1)} %pad_maximum_fusion.9), channel_id=1, source_target_pairs={{0,1},{1,0},{2,3},{3,2},{4,5},{5,4},{6,7},{7,6},{8,9},{9,8},{10,11... | collective-permute-start | bytes 1572872 | tf_op jit(solution)/shard_map/ppermute | solution.py:249
  102.9 11.6 %collective-permute-start.40 = (bf16[4,32,2048]{2,1,0:T(8,128)(2,1)S(1)}, bf16[4,32,2048]{2,1,0:T(8,128)(2,1)S(1)}, u32[]{:S(2)}, u32[]{:S(2)}) collective-permute-start(bf16[4,32,2048]{2,1,0:T(8,128)(2,1)S(1)} %pad_maximum_fusion.10), channel_id=1, source_target_pairs={{0,1},{1,0},{2,3},{3,2},{4,5},{5,4},{6,7},{7,6},{8,9},{9,8},{10,11... | collective-permute-start | bytes 1572872 | tf_op jit(solution)/shard_map/ppermute | solution.py:249
  103.4 8.4 %collective-permute-start.31 = (bf16[2,32,2048]{2,1,0:T(8,128)(2,1)S(1)}, bf16[2,32,2048]{2,1,0:T(8,128)(2,1)S(1)}, u32[]{:S(2)}, u32[]{:S(2)}) collective-permute-start(bf16[2,32,2048]{2,1,0:T(8,128)(2,1)S(1)} %slice.384), channel_id=1, source_target_pairs={{0,2},{1,3},{2,0},{3,1},{4,6},{5,7},{6,4},{7,5},{8,10},{9,11},{10,... | collective-permute-start | bytes 786440 | tf_op jit(solution)/shard_map/ppermute | solution.py:249
  111.9 14.5 %collective-permute-start.34 = (bf16[1,32,2048]{2,1,0:T(8,128)(2,1)S(1)}, bf16[1,32,2048]{2,1,0:T(8,128)(2,1)S(1)}, u32[]{:S(2)}, u32[]{:S(2)}) collective-permute-start(bf16[1,32,2048]{2,1,0:T(8,128)(2,1)S(1)} %slice.387), channel_id=1, source_target_pairs={{0,2},{1,3},{2,0},{3,1},{4,6},{5,7},{6,4},{7,5},{8,10},{9,11},{10,... | collective-permute-start | bytes 393224 | tf_op jit(solution)/shard_map/ppermute | solution.py:249
  112.7 23.2 %collective-permute-start.33 = (bf16[1,32,2048]{2,1,0:T(8,128)(2,1)S(1)}, bf16[1,32,2048]{2,1,0:T(8,128)(2,1)S(1)}, u32[]{:S(2)}, u32[]{:S(2)}) collective-permute-start(bf16[1,32,2048]{2,1,0:T(8,128)(2,1)S(1)} %slice.388), channel_id=1, source_target_pairs={{0,4},{1,5},{2,6},{3,7},{4,0},{5,1},{6,2},{7,3},{8,12},{9,13},{10,... | collective-permute-start | bytes 393224 | tf_op jit(solution)/shard_map/ppermute | solution.py:249
  122.9 2.9 %collective-permute-start.41 = (bf16[4,32,2048]{2,1,0:T(8,128)(2,1)S(1)}, bf16[4,32,2048]{2,1,0:T(8,128)(2,1)S(1)}, u32[]{:S(2)}, u32[]{:S(2)}) collective-permute-start(bf16[4,32,2048]{2,1,0:T(8,128)(2,1)S(1)} %bitcast.171), channel_id=1, source_target_pairs={{0,1},{1,0},{2,3},{3,2},{4,5},{5,4},{6,7},{7,6},{8,9},{9,8},{10,11... | collective-permute-start | bytes 1572872 | tf_op jit(solution)/shard_map/ppermute | solution.py:249
  123.0 2.6 %collective-permute-start.42 = (bf16[4,32,2048]{2,1,0:T(8,128)(2,1)S(1)}, bf16[4,32,2048]{2,1,0:T(8,128)(2,1)S(1)}, u32[]{:S(2)}, u32[]{:S(2)}) collective-permute-start(bf16[4,32,2048]{2,1,0:T(8,128)(2,1)S(1)} %bitcast.172), channel_id=1, source_target_pairs={{0,1},{1,0},{2,3},{3,2},{4,5},{5,4},{6,7},{7,6},{8,9},{9,8},{10,11... | collective-permute-start | bytes 1572872 | tf_op jit(solution)/shard_map/ppermute | solution.py:249
  125.9 8.4 %collective-permute-start.44 = (bf16[2,32,2048]{2,1,0:T(8,128)(2,1)S(1)}, bf16[2,32,2048]{2,1,0:T(8,128)(2,1)S(1)}, u32[]{:S(2)}, u32[]{:S(2)}) collective-permute-start(bf16[2,32,2048]{2,1,0:T(8,128)(2,1)S(1)} %slice.381), channel_id=1, source_target_pairs={{0,4},{1,5},{2,6},{3,7},{4,0},{5,1},{6,2},{7,3},{8,12},{9,13},{10,... | collective-permute-start | bytes 786440 | tf_op jit(solution)/shard_map/ppermute | solution.py:249
  126.4 8.1 %collective-permute-start.43 = (bf16[2,32,2048]{2,1,0:T(8,128)(2,1)S(1)}, bf16[2,32,2048]{2,1,0:T(8,128)(2,1)S(1)}, u32[]{:S(2)}, u32[]{:S(2)}) collective-permute-start(bf16[2,32,2048]{2,1,0:T(8,128)(2,1)S(1)} %slice.382), channel_id=1, source_target_pairs={{0,2},{1,3},{2,0},{3,1},{4,6},{5,7},{6,4},{7,5},{8,10},{9,11},{10,... | collective-permute-start | bytes 786440 | tf_op jit(solution)/shard_map/ppermute | solution.py:249
  134.6 5.0 %collective-permute-start.46 = (bf16[1,32,2048]{2,1,0:T(8,128)(2,1)S(1)}, bf16[1,32,2048]{2,1,0:T(8,128)(2,1)S(1)}, u32[]{:S(2)}, u32[]{:S(2)}) collective-permute-start(bf16[1,32,2048]{2,1,0:T(8,128)(2,1)S(1)} %slice.385), channel_id=1, source_target_pairs={{0,2},{1,3},{2,0},{3,1},{4,6},{5,7},{6,4},{7,5},{8,10},{9,11},{10,... | collective-permute-start | bytes 393224 | tf_op jit(solution)/shard_map/ppermute | solution.py:249
  136.0 5.0 %collective-permute-start.45 = (bf16[1,32,2048]{2,1,0:T(8,128)(2,1)S(1)}, bf16[1,32,2048]{2,1,0:T(8,128)(2,1)S(1)}, u32[]{:S(2)}, u32[]{:S(2)}) collective-permute-start(bf16[1,32,2048]{2,1,0:T(8,128)(2,1)S(1)} %slice.386), channel_id=1, source_target_pairs={{0,4},{1,5},{2,6},{3,7},{4,0},{5,1},{6,2},{7,3},{8,12},{9,13},{10,... | collective-permute-start | bytes 393224 | tf_op jit(solution)/shard_map/ppermute | solution.py:249
  141.3 14.5 %collective-permute-start.4 = (bf16[128,2048]{1,0:T(8,128)(2,1)S(1)}, bf16[128,2048]{1,0:T(8,128)(2,1)S(1)}, u32[]{:S(2)}, u32[]{:S(2)}) collective-permute-start(bf16[128,2048]{1,0:T(8,128)(2,1)S(1)} %param.7), channel_id=1, source_target_pairs={{0,0},{8,24},{16,16},{24,8},{1,1},{9,25},{17,17},{25,9},{2,2},{10,... | collective-permute-start | bytes 1572872 | tf_op jit(solution)/shard_map/cond/branch_5_fun/ppermute | solution.py:290
  (10 other events, 45.3 us)
